TPU v7x, 256 devices: a whole 4x4x8 slice. The times are simulated.
256 devices in a mesh: chan: 64 (over x, y, z_hi, core), beam: 4 (over z_lo).
Axes of the slice: x: 4, y: 4, z: 8 (z_hi: 2, z_lo: 4; z = z_hi * 4 + z_lo), core: 2. Of those that a mesh axis runs over, the one named last changes fastest.
Arguments:
- images: float32 [256, 36, 128, 128], P('chan', 'beam')
- beam_weight: float32 [36, 128, 128], P('beam'), may hold values from 0.2 to 1
- offsets: int32 [36, 2], P('beam'), may hold values from 0 to 384, as said below
- rejected_indicator: int32 [256, 192, 512], P('chan', None, 'beam'), may hold values 0 or 1
- regression_indicator: int32 [256], replicated, may hold values 0 or 1
Outputs:
- cleaned_cube: float32 [256, 192, 512], P(None, 'chan', 'beam')
Inputs may be any that keep to these rules, and one draw needn't show every extreme that they name: `offsets`: beam b = 6 r + q sits near row r * 64 // 5 and column q * 384 // 5, within 16; every sky pixel is covered by some beam; the first and last row and column of beams lie at the field's edges.
All inputs are finite; a program needn't handle non-finite values. No bound on the sum of `rejected_indicator` on one device may be relied on, other than what follows from the above.
Results may differ from a plain program's by a relative error of at most 0.00023.
Values sent between devices are 32-bit elements; how exact they have to be, the bound alone decides.
No kernel may reach another device: no remote copies, remote signals or barrier semaphores. Data moves between devices by JAX's collectives and lax.ppermute only.
A program may use at most 128 MiB of HBM per device.

v0:
```python
import jax
import jax.numpy as jnp
from jax import lax
from jax.sharding import PartitionSpec as P

MOS_ROWS = 192
MOS_COLS = 512


def legendre(count):
    position = (2.0 * jnp.arange(count).astype(jnp.float32) + 1.0) / count - 1.0
    square = position * position
    return jnp.stack(
        [
            jnp.ones_like(position),
            position,
            0.5 * (3.0 * square - 1.0),
            0.5 * (5.0 * square * position - 3.0 * position),
        ],
        axis=1,
    )


def solve_cubic(normal_matrix, right_side):
    factor = {}
    for outer in range(4):
        for inner in range(outer + 1):
            value = normal_matrix[outer * 4 + inner]
            for other in range(inner):
                value = value - factor[outer, other] * factor[inner, other]
            if outer == inner:
                factor[outer, outer] = jnp.sqrt(value)
            else:
                factor[outer, inner] = value / factor[inner, inner]
    forward = []
    for outer in range(4):
        value = right_side[outer]
        for other in range(outer):
            value = value - factor[outer, other] * forward[other]
        forward.append(value / factor[outer, outer])
    backward = [None] * 4
    for outer in range(3, -1, -1):
        value = forward[outer]
        for other in range(outer + 1, 4):
            value = value - factor[other, outer] * backward[other]
        backward[outer] = value / factor[outer, outer]
    return jnp.stack(backward, axis=0)


def clean_pair(pair):
    sky_tile, weight_tile = pair
    channels, rows, columns = sky_tile.shape
    celestial_image = sky_tile.reshape(channels, rows * columns)
    importance_factor = weight_tile.reshape(channels, rows * columns)
    table = legendre(channels)
    products = jnp.stack(
        [table[:, outer] * table[:, inner] for outer in range(4) for inner in range(4)], axis=0
    )
    normal_matrix = jnp.dot(
        products,
        importance_factor,
        precision=lax.Precision.HIGHEST,
        preferred_element_type=jnp.float32,
    )
    right_side = jnp.dot(
        table.T,
        importance_factor * celestial_image,
        precision=lax.Precision.HIGHEST,
        preferred_element_type=jnp.float32,
    )
    coefficients = solve_cubic(normal_matrix, right_side)
    continuum = jnp.dot(
        table, coefficients, precision=lax.Precision.HIGHEST, preferred_element_type=jnp.float32
    )
    residual = celestial_image - continuum
    padded = jnp.pad(residual, ((1, 1), (0, 0)))
    smoothed = 0.25 * padded[:-2] + 0.5 * residual + 0.25 * padded[2:]
    return smoothed.reshape(channels, rows, columns)


def place(values, row_start, col_start, side, columns, first_column):
    row_hit = (
        lax.broadcasted_iota(jnp.int32, (1, MOS_ROWS, side), 1)
        == lax.broadcasted_iota(jnp.int32, (1, MOS_ROWS, side), 2) + row_start[:, None, None]
    ).astype(jnp.float32)
    col_hit = (
        lax.broadcasted_iota(jnp.int32, (1, side, columns), 2) + first_column
        == lax.broadcasted_iota(jnp.int32, (1, side, columns), 1) + col_start[:, None, None]
    ).astype(jnp.float32)
    rows_placed = jnp.einsum(
        "bri,cbij->bcrj",
        row_hit,
        values,
        precision=lax.Precision.HIGHEST,
        preferred_element_type=jnp.float32,
    )
    return jnp.einsum(
        "bcrj,bjk->crk",
        rows_placed,
        col_hit,
        precision=lax.Precision.HIGHEST,
        preferred_element_type=jnp.float32,
    )


def local(images, beam_weight, offsets, rejected_indicator, regression_indicator):
    ch_dev = images.shape[0]
    side = images.shape[2]
    col_dev = rejected_indicator.shape[2]
    all_channels = regression_indicator.shape[0]
    first_channel = lax.axis_index("chan") * ch_dev
    channel_ids = first_channel + jnp.arange(ch_dev, dtype=jnp.int32)
    exponent = 1.0 + 0.5 * channel_ids.astype(jnp.float32) / (all_channels - 1)
    row_start = jnp.clip(offsets[:, 0], 0, MOS_ROWS - side)
    col_start = jnp.clip(offsets[:, 1], 0, MOS_COLS - side)
    log_weight = jnp.log(beam_weight)
    core = lax.axis_index("chan") % 2
    half = side // 2
    own_half = lax.dynamic_slice_in_dim(log_weight, core * half, half, 1)
    corner = jnp.zeros((log_weight.shape[0], 8, side), jnp.float32)
    corner = corner.at[:, 0, 0].set(row_start.astype(jnp.float32))
    corner = corner.at[:, 0, 1].set(col_start.astype(jnp.float32))
    shared = lax.all_gather(jnp.concatenate([own_half, corner], axis=1), "beam", axis=0, tiled=True)
    chan_size = lax.psum(1, "chan")
    other = lax.ppermute(shared, "chan", [(a, a ^ 1) for a in range(chan_size)])
    first_half = jnp.where(core == 0, shared, other)
    second_half = jnp.where(core == 0, other, shared)
    every_log = jnp.concatenate([first_half[:, :half], second_half[:, :half]], axis=1)
    every_row = first_half[:, half, 0].astype(jnp.int32)
    every_col = first_half[:, half, 1].astype(jnp.int32)
    response = jnp.exp(exponent[:, None, None, None] * log_weight[None])
    numerator = place(response * images, row_start, col_start, side, MOS_COLS, 0)
    dividend_accumulator = lax.psum_scatter(numerator, "beam", scatter_dimension=2, tiled=True)
    every_response = jnp.exp(exponent[:, None, None, None] * every_log[None])
    col_first = lax.axis_index("beam") * col_dev
    normalizer_accumulated = place(
        every_response * every_response, every_row, every_col, side, col_dev, col_first
    )
    accepted_entries = 1.0 - rejected_indicator.astype(jnp.float32)
    emission_absent = lax.dynamic_slice_in_dim(regression_indicator, first_channel, ch_dev).astype(
        jnp.float32
    )
    celestial_image = accepted_entries * dividend_accumulator / normalizer_accumulated
    importance_factor = normalizer_accumulated * (
        emission_absent[:, None, None] * accepted_entries + 0.01
    )
    arrived = lax.all_to_all(
        jnp.stack([celestial_image, importance_factor]),
        "chan",
        split_axis=2,
        concat_axis=1,
        tiled=True,
    )
    return clean_pair((arrived[0], arrived[1]))


def solution(mesh):
    in_specs = (
        P("chan", "beam", None, None),
        P("beam", None, None),
        P("beam", None),
        P("chan", None, "beam"),
        P(),
    )
    out_specs = P(None, "chan", "beam")
    return jax.shard_map(local, mesh=mesh, in_specs=in_specs, out_specs=out_specs, check_vma=False)
```

profile of v0, /device:TPU:33, one launch (start us, length us, event | category | flops | bytes accessed | tf_op | source)
XLA Modules:
  0.0 153.1 jit_solution(11954396857030517619)
XLA Ops:
  6.5 0.0 copy-start.1
  6.5 0.0 all-gather.2.cloned.1.call-start
  6.5 1.3 log.3
  7.8 0.8 fusion.76
  8.6 0.6 fusion.83
  9.2 1.2 scatter.9
  10.5 0.2 copy.16
  10.7 0.8 pad_maximum_fusion.2
  11.4 0.0 all-gather.2.cloned.1.call-update
  11.5 0.0 reduce-scatter.2.cloned.1.call-start
  11.5 0.0 copy-done.1
  11.5 2.3 %fusion.12 = f32[9,4,128,192]{2,3,0,1:T(8,128)S(1)} fusion(f32[4,9,128,128]{3,2,1,0:T(8,128)S(1)} %copy-done.1, f32[9,128,128]{2,1,0:T(8,128)S(1)} %log.3, f32[4]{0:T(128)S(1)} %multiply_add_fusion.3, s32[9]{0:T(128)S(1)} %get-tuple-element.51), kind=kOutput, calls=%fused_computation.15 | convolution fusion | flops 1360576512 | bytes 6488116 | tf_op jit(solution)/shard_map/bri,cbij->bcrj/dot_general | solution.py:90
  13.9 0.0 copy-start.3
  13.9 4.6 %fusion.21 = f32[4,192,512]{2,1,0:T(8,128)} fusion(f32[9,4,128,192]{2,3,0,1:T(8,128)S(1)} %fusion.12, s32[9]{0:T(128)S(1)} %get-tuple-element.48), kind=kOutput, calls=%fused_computation.22 | convolution fusion | flops 5436997632 | bytes 5111844 | tf_op jit(solution)/shard_map/bcrj,bjk->crk/dot_general | solution.py:97
  18.5 0.0 reduce-scatter.2.cloned.1.call-update
  18.5 31.4 %all-gather.2.cloned.1.call-done = f32[36,72,128]{2,1,0:T(8,128)} async-done(((f32[9,72,128]{2,1,0:T(8,128)}), f32[36,72,128]{2,1,0:T(8,128)}) %all-gather.2.cloned.1.call-update) | async-done | bytes 1327120 | tf_op jit(solution)/shard_map/all_gather | solution.py:123
  49.9 1.4 collective-permute-start
  51.3 0.0 copy-done.3
  51.3 0.1 dynamic-slice_convert_fusion
  51.4 2.8 %collective-permute-done = f32[36,72,128]{2,1,0:T(8,128)S(1)} collective-permute-done((f32[36,72,128]{2,1,0:T(8,128)}, f32[36,72,128]{2,1,0:T(8,128)S(1)}, u32[]{:S(2)}, u32[]{:S(2)}) %collective-permute-start) | collective-permute-done | bytes 1327136 | tf_op jit(solution)/shard_map/ppermute | solution.py:125
  54.2 0.1 broadcast_select_fusion
  54.3 0.1 slice.145
  54.5 1.4 fusion.46
  55.9 0.0 copy-done
  55.9 0.2 slice_select_fusion
  56.1 0.2 pad_maximum_fusion
  56.3 0.0 copy-start.2
  56.3 11.5 %fusion.2 = f32[36,4,128,192]{2,3,0,1:T(8,128)} fusion(f32[36,128,128]{2,1,0:T(8,128)S(1)} %pad_maximum_fusion, f32[4]{0:T(128)S(1)} %multiply_add_fusion.3, s32[36]{0:T(128)S(1)} %get-tuple-element.30), kind=kOutput, calls=%fused_computation.2 | convolution fusion | flops 5442306048 | bytes 16515232 | tf_op jit(solution)/shard_map/bri,cbij->bcrj/dot_general | solution.py:90
  67.7 24.5 %reduce-scatter.2.cloned.1.call-done = f32[4,192,128]{2,1,0:T(8,128)} async-done(((f32[4,192,512]{2,1,0:T(8,128)}), f32[4,192,128]{2,1,0:T(8,128)}) %reduce-scatter.2.cloned.1.call-update) | async-done | bytes 393232 | tf_op jit(solution)/shard_map/reduce_scatter | solution.py:133
  92.2 0.0 copy-done.2
  92.2 10.1 %divide_bitcast_fusion = (f32[1,4,192,128]{3,2,1,0:T(8,128)S(1)}, f32[1,4,192,128]{3,2,1,0:T(8,128)S(1)}) fusion(f32[4,192,128]{2,1,0:T(8,128)} %reduce-scatter.2.cloned.1.call-done, s32[4,192,128]{2,1,0:T(8,128)S(1)} %copy-done.2, f32[4]{0:T(128)S(1)} %dynamic-slice_convert_fusion, s32[36]{0:T(128)S(1)} %get-tuple-element.29, s32[128]{0:T(128)S(1)} %iota_add_fusion, ...), kind=kOutput, calls=%fused_computation.43 | convolution fusion | flops 5437685760 | bytes 15729312 | tf_op jit(solution)/shard_map/bcrj,bjk->crk/dot_general | solution.py:97
  102.4 0.1 pad_maximum_fusion.1
  102.4 1.4 copy.17
  103.9 12.4 %all-to-all-start = ((f32[2,4,192,128]{3,1,0,2:T(4,128)}), f32[2,4,192,128]{3,1,0,2:T(4,128)S(1)}, u32[]{:S(2)}, u32[]{:S(2)}) async-start(f32[2,4,192,128]{3,1,0,2:T(4,128)} %copy.17), calls=%async_computation.1 | async-start | bytes 1572864 | tf_op jit(solution)/shard_map/all_to_all | solution.py:147
  116.3 0.1 stack.16
  116.4 26.7 %all-to-all-done = f32[2,4,192,128]{3,1,0,2:T(4,128)S(1)} async-done(((f32[2,4,192,128]{3,1,0,2:T(4,128)}), f32[2,4,192,128]{3,1,0,2:T(4,128)S(1)}, u32[]{:S(2)}, u32[]{:S(2)}) %all-to-all-start) | async-done | bytes 786464 | tf_op jit(solution)/shard_map/all_to_all | solution.py:147
  143.1 0.1 copy.18
  143.3 0.1 fusion.82
  143.4 0.1 copy.19
  143.5 0.1 copy.20
  143.6 0.3 fusion.39
  143.9 0.3 fusion.41
  144.2 0.1 fusion.64
  144.4 0.1 subtract_divide_fusion
  144.4 0.7 convolution_subtract_fusion
  145.1 0.1 multiply_add_fusion
  145.2 0.2 copy.21
  145.4 0.9 copy.22
  (16 shorter events, 0.2 us)
Async XLA Ops:
  6.5 5.0 %copy-start.1 = (f32[4,9,128,128]{3,2,1,0:T(8,128)S(1)}, f32[4,9,128,128]{3,2,1,0:T(8,128)}, u32[]{:S(2)}) copy-start(f32[4,9,128,128]{3,2,1,0:T(8,128)} %param.9) | copy-start | bytes 7077892
  6.5 43.3 %all-gather.2.cloned.1.call-start = ((), (), s32[]{:S(2)}) async-start(), calls=%async_computation.3 | async-start | bytes 1658880 | tf_op jit(solution)/shard_map/all_gather | solution.py:123
  11.5 80.8 %reduce-scatter.2.cloned.1.call-start = ((), (), s32[]{:S(2)}) async-start(), calls=%async_computation.2 | async-start | bytes 1966080 | tf_op jit(solution)/shard_map/reduce_scatter | solution.py:133
  13.9 37.4 %copy-start.3 = (s32[256]{0:T(256)S(1)}, s32[256]{0:T(256)}, u32[]{:S(2)}) copy-start(s32[256]{0:T(256)} %param.13) | copy-start | bytes 3076
  49.9 4.3 %collective-permute-start = (f32[36,72,128]{2,1,0:T(8,128)}, f32[36,72,128]{2,1,0:T(8,128)S(1)}, u32[]{:S(2)}, u32[]{:S(2)}) collective-permute-start(f32[36,72,128]{2,1,0:T(8,128)} %all-gather.2.cloned.1.call-done), channel_id=1, source_target_pairs={{0,4},{4,0},{8,12},{12,8},{16,20},{20,16},{24,28},{28,24},{32,36},... | collective-permute-start | bytes 3981320 | tf_op jit(solution)/shard_map/ppermute | solution.py:125
  51.4 4.5 %copy-start = (f32[36,72,128]{2,1,0:T(8,128)S(1)}, f32[36,72,128]{2,1,0:T(8,128)}, u32[]{:S(2)}) copy-start(f32[36,72,128]{2,1,0:T(8,128)} %all-gather.2.cloned.1.call-done) | copy-start | bytes 3981316
  56.3 36.0 %copy-start.2 = (s32[4,192,128]{2,1,0:T(8,128)S(1)}, s32[4,192,128]{2,1,0:T(8,128)}, u32[]{:S(2)}) copy-start(s32[4,192,128]{2,1,0:T(8,128)} %param.12) | copy-start | bytes 1179652
  103.9 39.3 %all-to-all-start = ((f32[2,4,192,128]{3,1,0,2:T(4,128)}), f32[2,4,192,128]{3,1,0,2:T(4,128)S(1)}, u32[]{:S(2)}, u32[]{:S(2)}) async-start(f32[2,4,192,128]{3,1,0,2:T(4,128)} %copy.17), calls=%async_computation.1 | async-start | bytes 1572864 | tf_op jit(solution)/shard_map/all_to_all | solution.py:147
Sparse Core Ops, SparseCore 0:
  11.6 38.2 all-gather.1
  52.4 39.7 reduce-scatter.1
where the time goes:
time: 153 us
  waiting for transfers between devices  85.5 us (56%)
  matrix products  29.8 us (19%)
  starting transfers between devices  13.8 us (9%)
  between operations  13.6 us (9%)
  local copies, waits for them, and re-layouts  6.56 us (4%)
  other arithmetic  3.96 us (3%)
    all_gather x1, waiting for transfers between devices, local(): lax.all_gather(jnp.concatenate([own_half, corner], axis=1), 'beam', axis=...  31.4 us
    all_to_all x1, waiting for transfers between devices, local(): lax.all_to_all(jnp.stack([celestial_image, importance_factor]), 'chan', s...  26.7 us
    reduce_scatter x1, waiting for transfers between devices, local(): lax.psum_scatter(numerator, 'beam', scatter_dimension=2, tiled=True)  24.5 us
    dot_general x2, matrix products, place(): jnp.einsum('bcrj,bjk->crk', rows_placed, col_hit, precision=lax.Precision...  14.8 us
    dot_general x2, matrix products, place(): jnp.einsum('bri,cbij->bcrj', row_hit, values, precision=lax.Precision.HIG...  13.8 us
    all_to_all x1, starting transfers between devices, local(): lax.all_to_all(jnp.stack([celestial_image, importance_factor]), 'chan', s...  12.4 us
  transfers between devices with their start and end apart: 4, of which 4 were waited for; matrix products, arithmetic and copies ran while one was open for 14% of the time, Pallas kernels for 0%

commit v1 on v0

--- a/solution.py
+++ b/solution.py
@@ -120,7 +120,15 @@
     corner = jnp.zeros((log_weight.shape[0], 8, side), jnp.float32)
     corner = corner.at[:, 0, 0].set(row_start.astype(jnp.float32))
     corner = corner.at[:, 0, 1].set(col_start.astype(jnp.float32))
-    shared = lax.all_gather(jnp.concatenate([own_half, corner], axis=1), "beam", axis=0, tiled=True)
+    shared = jnp.concatenate(
+        lax.all_to_all(
+            jnp.stack([jnp.concatenate([own_half, corner], axis=1)] * lax.axis_size("beam")),
+            "beam",
+            0,
+            0,
+        ),
+        axis=0,
+    )
     chan_size = lax.psum(1, "chan")
     other = lax.ppermute(shared, "chan", [(a, a ^ 1) for a in range(chan_size)])
     first_half = jnp.where(core == 0, shared, other)

time: 153 us -> 146 us (0.954)
  the two profiles are of different devices: /device:TPU:33 before, /device:TPU:1 now
where the time goes in v1:
time: 146 us
  waiting for transfers between devices  64 us (44%)
  matrix products  31.5 us (22%)
  starting transfers between devices  25.8 us (18%)
  between operations  13.6 us (9%)
  local copies, waits for them, and re-layouts  7.66 us (5%)
  other arithmetic  3.23 us (2%)
    all_to_all x1, waiting for transfers between devices, local(): lax.all_to_all(jnp.stack([jnp.concatenate([own_half, corner], axis=1)] *...  36.8 us
    all_to_all x1, waiting for transfers between devices, local(): lax.all_to_all(jnp.stack([celestial_image, importance_factor]), 'chan', s...  24.6 us
    dot_general x2, matrix products, place(): jnp.einsum('bri,cbij->bcrj', row_hit, values, precision=lax.Precision.HIG...  15.5 us
    dot_general x2, matrix products, place(): jnp.einsum('bcrj,bjk->crk', rows_placed, col_hit, precision=lax.Precision...  14.8 us
    all_to_all x1, starting transfers between devices, local(): lax.all_to_all(jnp.stack([celestial_image, importance_factor]), 'chan', s...  14 us
    all_to_all x1, starting transfers between devices, local(): lax.all_to_all(jnp.stack([jnp.concatenate([own_half, corner], axis=1)] *...  6.43 us
    ppermute x1, starting transfers between devices, local(): other = lax.ppermute(shared, 'chan', [(a, a ^ 1) for a in range(chan_size)])  5.38 us
  transfers between devices with their start and end apart: 4, of which 3 were waited for; matrix products, arithmetic and copies ran while one was open for 15% of the time, Pallas kernels for 0%

profile of v1, /device:TPU:1, one launch (start us, length us, event | category | flops | bytes accessed | tf_op | source)
XLA Modules:
  0.0 145.7 jit_solution(12271616327910466324)
XLA Ops:
  6.5 1.1 log.3
  7.7 0.8 fusion.76
  8.5 0.6 fusion.83
  9.1 1.3 scatter.9
  10.4 0.2 copy.24
  10.7 1.2 stack.14
  11.8 6.4 %all-to-all-start = ((f32[4,9,72,128]{3,2,1,0:T(8,128)}), f32[4,9,72,128]{3,2,1,0:T(8,128)S(1)}, u32[]{:S(2)}, u32[]{:S(2)}) async-start(f32[4,9,72,128]{3,2,1,0:T(8,128)} %stack.14), calls=%async_computation.1 | async-start | bytes 2654208 | tf_op jit(solution)/shard_map/all_to_all | solution.py:124
  18.2 0.0 reduce-scatter.2.cloned.1.call-start
  18.3 4.0 %fusion.12 = f32[9,4,128,192]{2,3,0,1:T(8,128)S(1)} fusion(f32[4,9,128,128]{3,2,1,0:T(8,128)} %param.9, f32[9,128,128]{2,1,0:T(8,128)S(1)} %log.3, f32[4]{0:T(128)S(1)} %multiply_add_fusion.3, s32[9]{0:T(128)S(1)} %get-tuple-element.51), kind=kOutput, calls=%fused_computation.15 | convolution fusion | flops 1360576512 | bytes 6488116 | tf_op jit(solution)/shard_map/bri,cbij->bcrj/dot_general | solution.py:90
  22.2 0.0 copy-start.1
  22.3 4.6 %fusion.21 = f32[4,192,512]{2,1,0:T(8,128)} fusion(f32[9,4,128,192]{2,3,0,1:T(8,128)S(1)} %fusion.12, s32[9]{0:T(128)S(1)} %get-tuple-element.48), kind=kOutput, calls=%fused_computation.22 | convolution fusion | flops 5436997632 | bytes 5111844 | tf_op jit(solution)/shard_map/bcrj,bjk->crk/dot_general | solution.py:97
  26.9 0.0 reduce-scatter.2.cloned.1.call-update
  26.9 36.8 %all-to-all-done = f32[4,9,72,128]{3,2,1,0:T(8,128)S(1)} async-done(((f32[4,9,72,128]{3,2,1,0:T(8,128)}), f32[4,9,72,128]{3,2,1,0:T(8,128)S(1)}, u32[]{:S(2)}, u32[]{:S(2)}) %all-to-all-start) | async-done | bytes 1327136 | tf_op jit(solution)/shard_map/all_to_all | solution.py:124
  63.6 5.4 %collective-permute-start = (f32[36,72,128]{2,1,0:T(8,128)S(1)}, f32[36,72,128]{2,1,0:T(8,128)S(1)}, u32[]{:S(2)}, u32[]{:S(2)}) collective-permute-start(f32[36,72,128]{2,1,0:T(8,128)S(1)} %bitcast.74), channel_id=1, source_target_pairs={{0,4},{4,0},{8,12},{12,8},{16,20},{20,16},{24,28},{28,24},{32,36},... | collective-permute-start | bytes 3981320 | tf_op jit(solution)/shard_map/ppermute | solution.py:133
  69.0 0.0 copy-done.1
  69.0 0.1 dynamic-slice_convert_fusion
  69.1 2.6 %collective-permute-done = f32[36,72,128]{2,1,0:T(8,128)S(1)} collective-permute-done((f32[36,72,128]{2,1,0:T(8,128)S(1)}, f32[36,72,128]{2,1,0:T(8,128)S(1)}, u32[]{:S(2)}, u32[]{:S(2)}) %collective-permute-start) | collective-permute-done | bytes 1327136 | tf_op jit(solution)/shard_map/ppermute | solution.py:133
  71.7 0.1 broadcast_select_fusion
  71.8 0.1 slice.145
  72.0 1.4 fusion.46
  73.4 0.2 slice_select_fusion
  73.6 0.2 pad_maximum_fusion
  73.8 0.0 copy-start
  73.8 11.5 %fusion.2 = f32[36,4,128,192]{2,3,0,1:T(8,128)} fusion(f32[36,128,128]{2,1,0:T(8,128)S(1)} %pad_maximum_fusion, f32[4]{0:T(128)S(1)} %multiply_add_fusion.3, s32[36]{0:T(128)S(1)} %get-tuple-element.30), kind=kOutput, calls=%fused_computation.2 | convolution fusion | flops 5442306048 | bytes 16515232 | tf_op jit(solution)/shard_map/bri,cbij->bcrj/dot_general | solution.py:90
  85.3 0.0 reduce-scatter.2.cloned.1.call-done
  85.3 0.0 copy-done
  85.3 10.2 %divide_bitcast_fusion = (f32[1,4,192,128]{3,2,1,0:T(8,128)S(1)}, f32[1,4,192,128]{3,2,1,0:T(8,128)S(1)}) fusion(f32[4,192,128]{2,1,0:T(8,128)} %reduce-scatter.2.cloned.1.call-done, s32[4,192,128]{2,1,0:T(8,128)S(1)} %copy-done, f32[4]{0:T(128)S(1)} %dynamic-slice_convert_fusion, s32[36]{0:T(128)S(1)} %get-tuple-element.29, s32[128]{0:T(128)S(1)} %iota_add_fusion, ...), kind=kOutput, calls=%fused_computation.43 | convolution fusion | flops 5437685760 | bytes 15729312 | tf_op jit(solution)/shard_map/bcrj,bjk->crk/dot_general | solution.py:97
  95.4 0.1 pad_maximum_fusion.1
  95.5 1.4 copy.25
  96.9 14.0 %all-to-all-start.1 = ((f32[2,4,192,128]{3,1,0,2:T(4,128)}), f32[2,4,192,128]{3,1,0,2:T(4,128)S(1)}, u32[]{:S(2)}, u32[]{:S(2)}) async-start(f32[2,4,192,128]{3,1,0,2:T(4,128)} %copy.25), calls=%async_computation.2 | async-start | bytes 1572864 | tf_op jit(solution)/shard_map/all_to_all | solution.py:155
  111.0 0.1 stack.19
  111.1 24.6 %all-to-all-done.1 = f32[2,4,192,128]{3,1,0,2:T(4,128)S(1)} async-done(((f32[2,4,192,128]{3,1,0,2:T(4,128)}), f32[2,4,192,128]{3,1,0,2:T(4,128)S(1)}, u32[]{:S(2)}, u32[]{:S(2)}) %all-to-all-start.1) | async-done | bytes 786464 | tf_op jit(solution)/shard_map/all_to_all | solution.py:155
  135.7 0.1 copy.26
  135.8 0.1 fusion.82
  135.9 0.1 copy.27
  136.1 0.1 copy.28
  136.2 0.3 fusion.39
  136.5 0.3 fusion.41
  136.8 0.1 fusion.64
  137.0 0.1 subtract_divide_fusion
  137.0 0.7 convolution_subtract_fusion
  137.7 0.1 multiply_add_fusion
  137.8 0.2 copy.29
  138.0 0.9 copy.30
  (16 shorter events, 0.2 us)
Async XLA Ops:
  11.8 51.8 %all-to-all-start = ((f32[4,9,72,128]{3,2,1,0:T(8,128)}), f32[4,9,72,128]{3,2,1,0:T(8,128)S(1)}, u32[]{:S(2)}, u32[]{:S(2)}) async-start(f32[4,9,72,128]{3,2,1,0:T(8,128)} %stack.14), calls=%async_computation.1 | async-start | bytes 2654208 | tf_op jit(solution)/shard_map/all_to_all | solution.py:124
  18.2 67.0 %reduce-scatter.2.cloned.1.call-start = ((), (), s32[]{:S(2)}) async-start(), calls=%async_computation.3 | async-start | bytes 1966080 | tf_op jit(solution)/shard_map/reduce_scatter | solution.py:141
  22.2 46.8 %copy-start.1 = (s32[256]{0:T(256)S(1)}, s32[256]{0:T(256)}, u32[]{:S(2)}) copy-start(s32[256]{0:T(256)} %param.13) | copy-start | bytes 3076
  63.6 8.1 %collective-permute-start = (f32[36,72,128]{2,1,0:T(8,128)S(1)}, f32[36,72,128]{2,1,0:T(8,128)S(1)}, u32[]{:S(2)}, u32[]{:S(2)}) collective-permute-start(f32[36,72,128]{2,1,0:T(8,128)S(1)} %bitcast.74), channel_id=1, source_target_pairs={{0,4},{4,0},{8,12},{12,8},{16,20},{20,16},{24,28},{28,24},{32,36},... | collective-permute-start | bytes 3981320 | tf_op jit(solution)/shard_map/ppermute | solution.py:133
  73.8 11.5 %copy-start = (s32[4,192,128]{2,1,0:T(8,128)S(1)}, s32[4,192,128]{2,1,0:T(8,128)}, u32[]{:S(2)}) copy-start(s32[4,192,128]{2,1,0:T(8,128)} %param.12) | copy-start | bytes 1179652
  96.9 38.8 %all-to-all-start.1 = ((f32[2,4,192,128]{3,1,0,2:T(4,128)}), f32[2,4,192,128]{3,1,0,2:T(4,128)S(1)}, u32[]{:S(2)}, u32[]{:S(2)}) async-start(f32[2,4,192,128]{3,1,0,2:T(4,128)} %copy.25), calls=%async_computation.2 | async-start | bytes 1572864 | tf_op jit(solution)/shard_map/all_to_all | solution.py:155
Sparse Core Ops, SparseCore 0:
  27.0 47.5 reduce-scatter.1
